TPU v7x, 128 devices: a whole 4x4x4 slice. The times are simulated.
128 devices in a mesh: seq: 16 (over x, y), resp: 8 (over z, core).
Axes of the slice: x: 4, y: 4, z: 4, core: 2. Of those that a mesh axis runs over, the one named last changes fastest.
Arguments:
- prompt_keys: bfloat16 [2, 2048, 1024], P(None, 'seq'), may hold values from -6.1 to 6.1
- prompt_values: bfloat16 [2, 2048, 1024], P(None, 'seq'), may hold values from -6 to 6
- resp_query: bfloat16 [16, 1024, 8192], P('resp', None, 'seq'), may hold values from -121 to 121
- resp_keys: bfloat16 [16, 1024, 1024], P('resp'), may hold values from -6 to 6
- resp_values: bfloat16 [16, 1024, 1024], P('resp'), may hold values from -6 to 6
- prompt_x: bfloat16 [2, 2048, 16384], P(None, 'seq', 'resp'), may hold values from -6 to 6
- prompt_dt: float32 [2, 256, 2048], P(None, 'resp', 'seq'), may hold values from 0 to 0.5, as said below
- prompt_b: bfloat16 [2, 2048, 128], P(None, 'seq'), may hold values from -6 to 6
- prompt_c: bfloat16 [2, 2048, 128], P(None, 'seq'), may hold values from -0.5 to 0.5
- resp_x: bfloat16 [16, 1024, 16384], P('resp', None, 'seq'), may hold values from -6 to 6
- resp_dt: float32 [16, 256, 1024], P('resp', 'seq'), may hold values from 0 to 0.5, as said below
- resp_b: bfloat16 [16, 1024, 128], P('resp'), may hold values from -6 to 6
- resp_c: bfloat16 [16, 1024, 128], P('resp'), may hold values from -0.5 to 0.5
- ssm_rate: float32 [256], replicated, may hold values from 0.7 to 1.4
- resp_group: int32 [16], P('resp'), may hold values from 0 to 1
- resp_len: int32 [16], P('resp'), may hold values from 1 to 1024, 10240 in all
Outputs:
- resp_attn_out: bfloat16 [16, 1024, 8192], P('resp', None, 'seq')
- resp_ssm_out: bfloat16 [16, 1024, 16384], P('resp', None, 'seq')
- prompt_ssm_out: bfloat16 [2, 2048, 16384], P(None, 'seq', 'resp')
Inputs may be any that keep to these rules, and one draw needn't show every extreme that they name: `prompt_dt`: positive step sizes. `resp_dt`: positive step sizes.
All inputs are finite; a program needn't handle non-finite values. No bound on the sum of `resp_len` on one device may be relied on, other than what follows from the above.
Results may differ from a plain program's by a relative error of at most 0.0048.
Values may be sent and summed in bfloat16 or wider, within the bound.
No kernel may reach another device: no remote copies, remote signals or barrier semaphores. Data moves between devices by JAX's collectives and lax.ppermute only.
A program may use at most 192 MiB of HBM per device.

v0:
```python
import math

import jax
import jax.numpy as jnp
from jax import lax
from jax.experimental import pallas as pl
from jax.experimental.pallas import tpu as pltpu
from jax.sharding import PartitionSpec as P

HDIM = 128
SP = 64
NST = 128
QS = 128


EPS = 1e-05


def from_behind(block, axis, distance):
    devices = range(lax.axis_size(axis))
    route = [(i - distance, i) for i in devices if i - distance in devices]
    return lax.ppermute(block, axis, route)


def broadcast(value, axis, source):
    kept = jnp.where(lax.axis_index(axis) == source, value, 0).astype(value.dtype)
    return lax.psum(kept, axis)


def block_pass(inputs, steps, b_rows, c_rows, rates, state):
    exponent = jnp.cumsum(-steps * rates[:, None], axis=1)
    width = inputs.shape[0]
    lower = lax.broadcasted_iota(jnp.int32, (width, width), 0) >= lax.broadcasted_iota(
        jnp.int32, (width, width), 1
    )
    spread = jnp.where(lower[None], exponent[:, :, None] - exponent[:, None, :], -jnp.inf)
    gram = jnp.dot(c_rows, b_rows.T, preferred_element_type=jnp.float32)
    mixing = (jnp.exp(spread) * gram[None] * steps[:, None, :]).astype(jnp.bfloat16)
    local = jnp.einsum("hts,shp->thp", mixing, inputs, preferred_element_type=jnp.float32)
    carried = jnp.einsum(
        "tn,hpn->thp", c_rows.astype(jnp.float32), state, precision=lax.Precision.HIGHEST
    )
    output = local + carried * jnp.exp(exponent).T[:, :, None]
    last = exponent[:, -1]
    weighted = (
        inputs.astype(jnp.float32) * (jnp.exp(last[:, None] - exponent) * steps).T[:, :, None]
    ).astype(jnp.bfloat16)
    fresh = jnp.einsum("thp,tn->hpn", weighted, b_rows, preferred_element_type=jnp.float32)
    return (output, jnp.exp(last)[:, None, None] * state + fresh, exponent)


def sequence_pass(inputs, steps, b_rows, c_rows, rates):
    window_extent = inputs.shape[0]
    heads = steps.shape[0]
    blocks = window_extent // QS
    xs = inputs.reshape(blocks, QS, heads, SP)
    ss = steps.reshape(heads, blocks, QS).transpose(1, 0, 2)
    bs = b_rows.reshape(blocks, QS, NST)
    cs = c_rows.reshape(blocks, QS, NST)

    def advance(carry, block):
        state, offset = carry
        out, state_next, exponent = block_pass(block[0], block[1], block[2], block[3], rates, state)
        return ((state_next, offset + exponent[:, -1]), (out, offset[:, None] + exponent))

    start = (jnp.zeros((heads, SP, NST), jnp.float32), jnp.zeros((heads,), jnp.float32))
    (final, total), (outs, decays_to) = lax.scan(advance, start, (xs, ss, bs, cs))
    decays_to = decays_to.transpose(1, 0, 2).reshape(heads, window_extent)
    return (outs.reshape(window_extent, heads, SP), final, decays_to, total)


def chunked_pass(inputs, steps, b_rows, c_rows, rates):
    window_extent = inputs.shape[0]
    heads = steps.shape[0]
    blocks = window_extent // QS
    xs = inputs.reshape(blocks, QS, heads, SP).transpose(0, 2, 1, 3)
    ss = steps.reshape(heads, blocks, QS).transpose(1, 0, 2)
    bs = b_rows.reshape(blocks, QS, NST)
    cs = c_rows.reshape(blocks, QS, NST)
    exponent = jnp.cumsum(-ss * rates[None, :, None], axis=2)
    lower = lax.broadcasted_iota(jnp.int32, (QS, QS), 0) >= lax.broadcasted_iota(
        jnp.int32, (QS, QS), 1
    )
    spread = jnp.where(
        lower[None, None], exponent[:, :, :, None] - exponent[:, :, None, :], -jnp.inf
    )
    gram = jnp.einsum("ctn,cun->ctu", cs, bs, preferred_element_type=jnp.float32)
    mixing = (jnp.exp(spread) * gram[:, None] * ss[:, :, None, :]).astype(jnp.bfloat16)
    local = jnp.einsum("chtu,chup->chtp", mixing, xs, preferred_element_type=jnp.float32)
    last = exponent[:, :, -1]
    weighted = (
        xs.astype(jnp.float32) * (jnp.exp(last[:, :, None] - exponent) * ss)[:, :, :, None]
    ).astype(jnp.bfloat16)
    fresh = jnp.einsum("chup,cun->chpn", weighted, bs, preferred_element_type=jnp.float32)
    decay = jnp.exp(last)
    state = jnp.zeros((heads, SP, NST), jnp.float32)
    offset = jnp.zeros((heads,), jnp.float32)
    befores = []
    offsets = []
    for index in range(blocks):
        befores.append(state)
        offsets.append(offset)
        state = decay[index][:, None, None] * state + fresh[index]
        offset = offset + last[index]
    before = jnp.stack(befores)
    carried = jnp.einsum(
        "ctn,chpn->chtp", cs.astype(jnp.float32), before, precision=lax.Precision.HIGHEST
    )
    output = local + carried * jnp.exp(exponent)[:, :, :, None]
    decays_to = jnp.stack(offsets)[:, :, None] + exponent
    output = output.transpose(0, 2, 1, 3).reshape(window_extent, heads, SP)
    decays_to = decays_to.transpose(1, 0, 2).reshape(heads, window_extent)
    return (output, state, decays_to, offset)


def head_norm(values):
    scale = lax.rsqrt(jnp.mean(values * values, axis=-1, keepdims=True) + EPS)
    return (values * scale).reshape(values.shape[0], -1)


def linkage_merge(earlier, later):
    return (earlier[0] * later[0], later[0][:, :, None, None] * earlier[1] + later[1])


def body(
    prompt_keys,
    prompt_values,
    resp_query,
    resp_keys,
    resp_values,
    prompt_x,
    prompt_dt,
    prompt_b,
    prompt_c,
    resp_x,
    resp_dt,
    resp_b,
    resp_c,
    ssm_rate,
    resp_group,
    resp_len,
):
    seq_index = lax.axis_index("seq")
    resp_index = lax.axis_index("resp")
    seq_count = lax.axis_size("seq")
    prompt_count = prompt_x.shape[0]
    prompt_heads = prompt_dt.shape[1]
    resp_heads = resp_dt.shape[1]
    responses_here = resp_x.shape[0]
    slots = resp_x.shape[1]
    memory_head_number = prompt_keys.shape[2] // HDIM
    repeat = seq_count // memory_head_number
    shard_rows = prompt_keys.shape[1]
    spread_keys = jnp.repeat(
        prompt_keys.reshape(prompt_count, shard_rows, memory_head_number, HDIM), repeat, axis=2
    ).reshape(prompt_count, shard_rows, seq_count * HDIM)
    spread_values = jnp.repeat(
        prompt_values.reshape(prompt_count, shard_rows, memory_head_number, HDIM), repeat, axis=2
    ).reshape(prompt_count, shard_rows, seq_count * HDIM)
    moved_keys, moved_values = (
        lax.all_to_all(spread_keys, "seq", split_axis=2, concat_axis=1, tiled=True),
        lax.all_to_all(spread_values, "seq", split_axis=2, concat_axis=1, tiled=True),
    )
    resp_rates = lax.dynamic_slice_in_dim(ssm_rate, seq_index * resp_heads, resp_heads)
    resp_count = lax.axis_size("resp")
    heads_per_chain = prompt_heads // seq_count
    halves = seq_count // resp_count
    width = heads_per_chain * SP
    shard_rows = prompt_x.shape[1]
    spread_x = prompt_x.reshape(prompt_count, shard_rows, halves, resp_count, width)
    spread_x = lax.all_to_all(spread_x, "resp", 3, 3, tiled=True)
    spread_x = spread_x.transpose(0, 1, 3, 2, 4).reshape(prompt_count, shard_rows, seq_count, width)
    chain_x = lax.all_to_all(spread_x, "seq", 2, 1, tiled=True).reshape(
        prompt_count, shard_rows * seq_count, width
    )
    spread_dt = prompt_dt.reshape(prompt_count, halves, resp_count, heads_per_chain, shard_rows)
    spread_dt = lax.all_to_all(spread_dt, "resp", 2, 2, tiled=True)
    spread_dt = spread_dt.transpose(0, 2, 1, 3, 4).reshape(
        prompt_count, seq_count, heads_per_chain, shard_rows
    )
    chain_dt = lax.all_to_all(spread_dt, "seq", 1, 3, tiled=True).reshape(
        prompt_count, heads_per_chain, shard_rows * seq_count
    )
    chain_b = lax.all_gather(prompt_b, "seq", axis=1, tiled=True)
    chain_c = lax.all_gather(prompt_c, "seq", axis=1, tiled=True)
    own_head = seq_index // repeat
    attention_args = (moved_keys, moved_values, resp_keys, resp_values, resp_group, resp_len, own_head)
    outs = []
    for item in range(responses_here):
        outs.append(response_attention(resp_query, *attention_args, item))
    chain_x, chain_dt, outs = lax.optimization_barrier((chain_x, chain_dt, outs))
    chain_rates = lax.dynamic_slice_in_dim(
        ssm_rate, seq_index * resp_heads + resp_index * heads_per_chain, heads_per_chain
    )
    chain_outs = []
    chain_finals = []
    for prompt in range(prompt_count):
        out, final, decays_to, total = chunked_pass(
            chain_x[prompt], chain_dt[prompt], chain_b[prompt], chain_c[prompt], chain_rates
        )
        chain_outs.append(head_norm(out).astype(jnp.bfloat16))
        chain_finals.append(final)
    chain_final, resp_x = lax.optimization_barrier((jnp.stack(chain_finals), resp_x))
    start_states = lax.all_gather(chain_final, "resp", axis=1, tiled=True)
    back = jnp.stack(chain_outs).reshape(prompt_count, shard_rows * seq_count, 1, width)
    back = lax.all_to_all(back, "seq", 1, 2, tiled=True)
    back = back.reshape(prompt_count, shard_rows, resp_count, halves, width).transpose(0, 1, 3, 2, 4)
    back = lax.all_to_all(back, "resp", 3, 3, tiled=True)
    prompt_ssm_out = back.reshape(prompt_count, shard_rows, halves * resp_count * width)
    resp_locals = []
    for item in range(responses_here):
        resp_locals.append(
            chunked_pass(resp_x[item], resp_dt[item], resp_b[item], resp_c[item], resp_rates)
        )
    start_states, resp_locals = lax.optimization_barrier((start_states, resp_locals))
    resp_attn_out = jnp.concatenate(outs, axis=0)
    positions = lax.broadcasted_iota(jnp.int32, (slots,), 0)
    resp_outs = []
    for item in range(responses_here):
        out, final, decays_to, total = resp_locals[item]
        initial = lax.dynamic_index_in_dim(start_states, resp_group[item], 0, keepdims=False)
        carried = jnp.einsum(
            "tn,hdn->thd",
            resp_c[item].astype(jnp.float32),
            initial,
            precision=lax.Precision.HIGHEST,
        )
        corrected = out + jnp.exp(decays_to).T[:, :, None] * carried
        valid = positions < resp_len[item]
        resp_outs.append(jnp.where(valid[:, None], head_norm(corrected), 0.0).astype(jnp.bfloat16))
    resp_ssm_out = jnp.stack(resp_outs)
    return (resp_attn_out, resp_ssm_out, prompt_ssm_out)


ROWS = 512

def response_attention(resp_query, prompt_keys, prompt_values, resp_keys, resp_values, group, length, head, which):
    _, slots, width = resp_query.shape
    items = 1
    heads = width // HDIM
    rows = slots * heads
    queries = resp_query.reshape(resp_query.shape[0], rows, HDIM)
    prompt_len = prompt_keys.shape[1]
    tile = min(ROWS, rows)
    scale = 1.0 / math.sqrt(HDIM)

    def kernel(group_ref, len_ref, head_ref, q_ref, pk_ref, pv_ref, rk_ref, rv_ref, o_ref):
        item = pl.program_id(0)
        block = pl.program_id(1)
        window_extent = len_ref[which + item]
        first = block * (tile // heads)

        @pl.when(first >= window_extent)
        def _():
            o_ref[...] = jnp.zeros_like(o_ref)

        @pl.when(first < window_extent)
        def _():
            q = q_ref[0]
            dims = (((1,), (1,)), ((), ()))
            s1 = lax.dot_general(q, pk_ref[0], dims, preferred_element_type=jnp.float32) * scale
            s2 = lax.dot_general(q, rk_ref[0], dims, preferred_element_type=jnp.float32) * scale
            position = first + lax.broadcasted_iota(jnp.int32, (tile, 1), 0) // heads
            column = lax.broadcasted_iota(jnp.int32, s2.shape, 1)
            s2 = jnp.where(column <= position, s2, -jnp.inf)
            top = jnp.maximum(
                jnp.max(s1, axis=1, keepdims=True), jnp.max(s2, axis=1, keepdims=True)
            )
            e1 = jnp.exp(s1 - top)
            e2 = jnp.exp(s2 - top)
            total = jnp.sum(e1, axis=1, keepdims=True) + jnp.sum(e2, axis=1, keepdims=True)
            mixed = jnp.dot(
                e1.astype(jnp.bfloat16), pv_ref[0], preferred_element_type=jnp.float32
            ) + jnp.dot(e2.astype(jnp.bfloat16), rv_ref[0], preferred_element_type=jnp.float32)
            mixed = mixed / total
            o_ref[0] = jnp.where(position < window_extent, mixed, 0.0).astype(o_ref.dtype)

    keys_total = prompt_len + slots
    cost = pl.CostEstimate(
        flops=4 * items * rows * keys_total * HDIM,
        transcendentals=items * rows * keys_total,
        bytes_accessed=2 * (2 * items * rows * HDIM + 2 * items * keys_total * HDIM),
    )
    grid_spec = pltpu.PrefetchScalarGridSpec(
        num_scalar_prefetch=3,
        grid=(items, rows // tile),
        in_specs=[
            pl.BlockSpec((1, tile, HDIM), lambda i, b, g, n, h: (which + i, b, 0)),
            pl.BlockSpec((1, prompt_len, HDIM), lambda i, b, g, n, h: (g[which + i], 0, 0)),
            pl.BlockSpec((1, prompt_len, HDIM), lambda i, b, g, n, h: (g[which + i], 0, 0)),
            pl.BlockSpec((1, slots, HDIM), lambda i, b, g, n, h: (which + i, 0, h[0])),
            pl.BlockSpec((1, slots, HDIM), lambda i, b, g, n, h: (which + i, 0, h[0])),
        ],
        out_specs=pl.BlockSpec((1, tile, HDIM), lambda i, b, g, n, h: (i, b, 0)),
    )
    out = pl.pallas_call(
        kernel,
        grid_spec=grid_spec,
        out_shape=jax.ShapeDtypeStruct((items, rows, HDIM), jnp.bfloat16),
        compiler_params=pltpu.CompilerParams(vmem_limit_bytes=60 * 1024 * 1024),
        cost_estimate=cost,
    )(group.astype(jnp.int32), length.astype(jnp.int32), jnp.reshape(head, (1,)).astype(jnp.int32),
      queries, prompt_keys, prompt_values, resp_keys, resp_values)
    return out.reshape(items, slots, width)


def solution(mesh):
    placed = (
        P(None, "seq", None),
        P(None, "seq", None),
        P("resp", None, "seq"),
        P("resp", None, None),
        P("resp", None, None),
        P(None, "seq", "resp"),
        P(None, "resp", "seq"),
        P(None, "seq", None),
        P(None, "seq", None),
        P("resp", None, "seq"),
        P("resp", "seq", None),
        P("resp", None, None),
        P("resp", None, None),
        P(),
        P("resp"),
        P("resp"),
    )
    return jax.shard_map(
        body,
        mesh=mesh,
        in_specs=placed,
        out_specs=(P("resp", None, "seq"), P("resp", None, "seq"), P(None, "seq", "resp")),
        check_vma=False,
    )
```

profile of v0, /device:TPU:1, one launch (start us, length us, event | category | flops | bytes accessed | tf_op | source)
XLA Modules:
  0.0 354.8 jit_solution(3364188191825978593)
XLA Ops:
  9.3 6.8 %all-to-all-start.2 = ((f32[2,2,8,2,128]{4,1,3,0,2:T(2,128)}), f32[2,2,8,2,128]{4,1,3,0,2:T(2,128)S(1)}, u32[]{:S(2)}, u32[]{:S(2)}) async-start(f32[2,2,8,2,128]{4,1,3,0,2:T(2,128)} %copy.154), calls=%async_computation.2 | async-start | bytes 65536 | tf_op jit(solution)/shard_map/all_to_all | solution.py:177
  27.4 6.8 %all-to-all-start.3 = ((f32[2,16,2,128]{3,2,0,1:T(2,128)}), f32[2,16,2,128]{3,2,0,1:T(2,128)S(1)}, u32[]{:S(2)}, u32[]{:S(2)}) async-start(f32[2,16,2,128]{3,2,0,1:T(2,128)} %copy.156), calls=%async_computation.3 | async-start | bytes 65536 | tf_op jit(solution)/shard_map/all_to_all | solution.py:181
  40.6 6.2 %all-to-all-start = ((bf16[2,128,2,8,128]{1,4,2,0,3:T(8,128)(2,1)}), bf16[2,128,2,8,128]{1,4,2,0,3:T(8,128)(2,1)S(1)}, u32[]{:S(2)}, u32[]{:S(2)}) async-start(bf16[2,128,2,8,128]{1,4,2,0,3:T(8,128)(2,1)} %copy.150), calls=%async_computation | async-start | bytes 2097152 | tf_op jit(solution)/shard_map/all_to_all | solution.py:171
  50.8 11.2 %all-to-all-done = bf16[2,128,2,8,128]{1,4,2,0,3:T(8,128)(2,1)S(1)} async-done(((bf16[2,128,2,8,128]{1,4,2,0,3:T(8,128)(2,1)}), bf16[2,128,2,8,128]{1,4,2,0,3:T(8,128)(2,1)S(1)}, u32[]{:S(2)}, u32[]{:S(2)}) %all-to-all-start) | async-done | bytes 1048608 | tf_op jit(solution)/shard_map/all_to_all | solution.py:171
  63.7 3.7 %all-to-all-start.4 = ((bf16[2,128,2048]{1,0,2:T(2,128)(2,1)}), bf16[2,128,2048]{1,0,2:T(2,128)(2,1)S(1)}, u32[]{:S(2)}, u32[]{:S(2)}) async-start(bf16[2,128,2048]{1,0,2:T(2,128)(2,1)} %bitcast.13), calls=%async_computation.4 | async-start | bytes 2097152 | tf_op jit(solution)/shard_map/all_to_all | solution.py:161
  73.8 10.3 %all-to-all-done.4 = bf16[2,128,2048]{1,0,2:T(2,128)(2,1)S(1)} async-done(((bf16[2,128,2048]{1,0,2:T(2,128)(2,1)}), bf16[2,128,2048]{1,0,2:T(2,128)(2,1)S(1)}, u32[]{:S(2)}, u32[]{:S(2)}) %all-to-all-start.4) | async-done | bytes 1048608 | tf_op jit(solution)/shard_map/all_to_all | solution.py:161
  85.8 4.4 %all-to-all-start.5 = ((bf16[2,128,2048]{1,0,2:T(2,128)(2,1)}), bf16[2,128,2048]{1,0,2:T(2,128)(2,1)S(1)}, u32[]{:S(2)}, u32[]{:S(2)}) async-start(bf16[2,128,2048]{1,0,2:T(2,128)(2,1)} %bitcast.394), calls=%async_computation.5 | async-start | bytes 2097152 | tf_op jit(solution)/shard_map/all_to_all | solution.py:162
  97.0 4.3 %reshape.680.q_ref = bf16[2,4096,128]{2,1,0:T(8,128)(2,1)} reshape(bf16[2,1024,512]{2,1,0:T(8,128)(2,1)} %param.18) | data formatting | bytes 4194304 | tf_op jit(solution)/shard_map/reshape | solution.py:242
  117.8 6.8 %all-to-all-start.1 = ((bf16[2,128,16,128]{3,1,0,2:T(8,128)(2,1)}), bf16[2,128,16,128]{3,1,0,2:T(8,128)(2,1)S(1)}, u32[]{:S(2)}, u32[]{:S(2)}) async-start(bf16[2,128,16,128]{3,1,0,2:T(8,128)(2,1)} %copy.152), calls=%async_computation.1 | async-start | bytes 2097152 | tf_op jit(solution)/shard_map/all_to_all | solution.py:173
  126.1 18.9 %shard_map.175 = bf16[1,4096,128]{2,1,0:T(8,128)(2,1)} custom-call(s32[2]{0:T(128)} %group_ref.3, s32[2]{0:T(128)} %len_ref.3, s32[1]{0:T(128)} %bitcast.11.head_ref, bf16[2,4096,128]{2,1,0:T(8,128)(2,1)} %reshape.680.q_ref, bf16[2,2048,128]{2,1,0:T(8,128)(2,1)} %bitcast.412, bf16[2,2048,128]{2,1,0:T(8,128)(2,1)} %bitcast.414, ...), custom_call_target="tpu_custom_call" | custom-call | flops 6442450944 | bytes 3670016 | tf_op jit(solution)/shard_map/pallas_call | solution.py:296
  146.7 34.5 %shard_map.176 = bf16[1,4096,128]{2,1,0:T(8,128)(2,1)} custom-call(s32[2]{0:T(128)} %group_ref.3, s32[2]{0:T(128)} %len_ref.3, s32[1]{0:T(128)} %bitcast.11.head_ref, bf16[2,4096,128]{2,1,0:T(8,128)(2,1)} %reshape.680.q_ref, bf16[2,2048,128]{2,1,0:T(8,128)(2,1)} %bitcast.413, bf16[2,2048,128]{2,1,0:T(8,128)(2,1)} %bitcast.415, ...), custom_call_target="tpu_custom_call" | custom-call | flops 6442450944 | bytes 3670016 | tf_op jit(solution)/shard_map/pallas_call | solution.py:296
  234.6 6.7 %all-to-all-start.6 = ((bf16[2,2048,1,128]{3,0,2,1:T(2,128)(2,1)}), bf16[2,2048,1,128]{3,0,2,1:T(2,128)(2,1)S(1)}, u32[]{:S(2)}, u32[]{:S(2)}) async-start(bf16[2,2048,1,128]{3,0,2,1:T(2,128)(2,1)} %copy.192), calls=%async_computation.6 | async-start | bytes 2097152 | tf_op jit(solution)/shard_map/all_to_all | solution.py:206
  242.1 4.1 %fusion.74 = (bf16[1,1024,1024]{2,1,0:T(8,128)(2,1)}, bf16[1,1024,1024]{2,1,0:T(8,128)(2,1)S(1)}) fusion(bf16[2,1024,1024]{2,1,0:T(8,128)(2,1)} %param.25), kind=kLoop, calls=%fused_computation.305 | loop fusion | bytes 8388608 | tf_op jit(solution)/shard_map/slice | solution.py:213
  246.2 6.3 %reshape.709 = bf16[8,128,16,64]{3,2,1,0:T(8,128)(2,1)} reshape(bf16[1,1024,1024]{2,1,0:T(8,128)(2,1)} %get-tuple-element.132) | data formatting | bytes 4194304 | tf_op jit(solution)/shard_map/reshape;squeeze | solution.py:76
  252.5 5.8 %copy.177 = bf16[8,128,16,64]{1,3,2,0:T(8,128)(2,1)} copy(bf16[8,128,16,64]{3,2,1,0:T(8,128)(2,1)} %reshape.709) | data formatting | bytes 4194304 | tf_op jit(solution)/shard_map/reshape;squeeze | solution.py:76
  258.3 3.9 %reshape.708 = bf16[8,128,16,64]{3,2,1,0:T(8,128)(2,1)} reshape(bf16[1,1024,1024]{2,1,0:T(8,128)(2,1)S(1)} %get-tuple-element.133) | data formatting | bytes 4194304 | tf_op jit(solution)/shard_map/reshape;squeeze | solution.py:76
  262.2 5.1 %copy.172 = bf16[8,128,16,64]{1,3,2,0:T(8,128)(2,1)S(1)} copy(bf16[8,128,16,64]{3,2,1,0:T(8,128)(2,1)} %reshape.708) | data formatting | bytes 4194304 | tf_op jit(solution)/shard_map/reshape;squeeze | solution.py:76
  272.3 3.1 fusion.1
  278.1 2.7 fusion.5
  284.7 3.0 fusion
  287.7 2.9 fusion.7
  294.4 31.4 %all-to-all-start.7 = ((bf16[2,128,2,8,128]{4,1,2,0,3:T(8,128)(2,1)}), bf16[2,128,2,8,128]{4,1,2,0,3:T(8,128)(2,1)S(1)}, u32[]{:S(2)}, u32[]{:S(2)}) async-start(bf16[2,128,2,8,128]{4,1,2,0,3:T(8,128)(2,1)} %copy.194), calls=%async_computation.7 | async-start | bytes 2097152 | tf_op jit(solution)/shard_map/all_to_all | solution.py:208
  325.9 4.8 %multiply_reduce_fusion.1 = (f32[1024,16]{0,1:T(8,128)S(1)}, f32[1024,16,64]{0,2,1:T(8,128)S(1)}) fusion(f32[1024,16,64]{0,2,1:T(8,128)} %bitcast.383, bf16[2,1024,128]{2,1,0:T(8,128)(2,1)S(1)} %copy-done.9, f32[2,16,64,128]{3,2,1,0:T(8,128)} %all-gather.6.cloned.1.call-done, s32[]{:T(128)S(6)} %select_n.58, f32[1024,16]{0,1:T(8,128)S(1)} %exponential_bitcast_fusion.1), kind=kOutput, calls=%fused_computation.20 | convolution fusion | flops 1614790656 | bytes 9306116 | tf_op jit(solution)/shard_map/tn,hdn->thd/dot_general | solution.py:222
  338.3 2.9 copy.181
  (368 shorter events, 138.7 us)
Async XLA Ops:
  7.2 202.9 %all-gather.4.cloned.1.call-start = ((), (), s32[]{:S(2)}) async-start(), calls=%async_computation.8 | async-start | bytes 1114112 | tf_op jit(solution)/shard_map/all_gather | solution.py:184
  9.3 17.4 %all-to-all-start.2 = ((f32[2,2,8,2,128]{4,1,3,0,2:T(2,128)}), f32[2,2,8,2,128]{4,1,3,0,2:T(2,128)S(1)}, u32[]{:S(2)}, u32[]{:S(2)}) async-start(f32[2,2,8,2,128]{4,1,3,0,2:T(2,128)} %copy.154), calls=%async_computation.2 | async-start | bytes 65536 | tf_op jit(solution)/shard_map/all_to_all | solution.py:177
  16.1 195.3 %all-gather.8.cloned.1.call-start = ((), (), s32[]{:S(2)}) async-start(), calls=%async_computation.10 | async-start | bytes 1114112 | tf_op jit(solution)/shard_map/all_gather | solution.py:185
  17.5 29.4 %copy-start.85 = (s32[2]{0:T(128)S(1)}, s32[2]{0:T(128)}, u32[]{:S(2)}) copy-start(s32[2]{0:T(128)} %len_ref.3) | copy-start | bytes 28
  17.5 30.0 %copy-start.17 = (bf16[2,128,1024]{2,1,0:T(8,128)(2,1)S(1)}, bf16[2,128,1024]{2,1,0:T(8,128)(2,1)}, u32[]{:S(2)}) copy-start(bf16[2,128,1024]{2,1,0:T(8,128)(2,1)} %param.16) | copy-start | bytes 1572868
  19.9 51.5 %copy-start.15 = (f32[2,8,8,128]{3,2,1,0:T(8,128)}, f32[2,8,8,128]{3,2,1,0:T(8,128)S(1)}, u32[]{:S(2)}) copy-start(f32[2,8,8,128]{3,2,1,0:T(8,128)S(1)} %copy.221) | copy-start | bytes 196612
  19.9 50.7 %copy-start.16 = (f32[2,8,8,128]{3,2,1,0:T(8,128)}, f32[2,8,8,128]{3,2,1,0:T(8,128)S(1)}, u32[]{:S(2)}) copy-start(f32[2,8,8,128]{3,2,1,0:T(8,128)S(1)} %copy.222) | copy-start | bytes 196612
  27.4 13.2 %all-to-all-start.3 = ((f32[2,16,2,128]{3,2,0,1:T(2,128)}), f32[2,16,2,128]{3,2,0,1:T(2,128)S(1)}, u32[]{:S(2)}, u32[]{:S(2)}) async-start(f32[2,16,2,128]{3,2,0,1:T(2,128)} %copy.156), calls=%async_computation.3 | async-start | bytes 65536 | tf_op jit(solution)/shard_map/all_to_all | solution.py:181
  40.6 29.3 %copy-start.30 = (f32[2,16,2,128]{3,2,0,1:T(2,128)}, f32[2,16,2,128]{3,2,0,1:T(2,128)S(1)}, u32[]{:S(2)}) copy-start(f32[2,16,2,128]{3,2,0,1:T(2,128)S(1)} %all-to-all-done.3) | copy-start | bytes 98308
  40.6 21.3 %all-to-all-start = ((bf16[2,128,2,8,128]{1,4,2,0,3:T(8,128)(2,1)}), bf16[2,128,2,8,128]{1,4,2,0,3:T(8,128)(2,1)S(1)}, u32[]{:S(2)}, u32[]{:S(2)}) async-start(bf16[2,128,2,8,128]{1,4,2,0,3:T(8,128)(2,1)} %copy.150), calls=%async_computation | async-start | bytes 2097152 | tf_op jit(solution)/shard_map/all_to_all | solution.py:171
  63.7 20.3 %all-to-all-start.4 = ((bf16[2,128,2048]{1,0,2:T(2,128)(2,1)}), bf16[2,128,2048]{1,0,2:T(2,128)(2,1)S(1)}, u32[]{:S(2)}, u32[]{:S(2)}) async-start(bf16[2,128,2048]{1,0,2:T(2,128)(2,1)} %bitcast.13), calls=%async_computation.4 | async-start | bytes 2097152 | tf_op jit(solution)/shard_map/all_to_all | solution.py:161
  73.8 27.6 %copy-start.91 = (f32[256]{0:T(256)S(1)}, f32[256]{0:T(256)}, u32[]{:S(2)}) copy-start(f32[256]{0:T(256)} %param.29) | copy-start | bytes 3076
  85.8 31.9 %all-to-all-start.5 = ((bf16[2,128,2048]{1,0,2:T(2,128)(2,1)}), bf16[2,128,2048]{1,0,2:T(2,128)(2,1)S(1)}, u32[]{:S(2)}, u32[]{:S(2)}) async-start(bf16[2,128,2048]{1,0,2:T(2,128)(2,1)} %bitcast.394), calls=%async_computation.5 | async-start | bytes 2097152 | tf_op jit(solution)/shard_map/all_to_all | solution.py:162
  117.8 66.0 %all-to-all-start.1 = ((bf16[2,128,16,128]{3,1,0,2:T(8,128)(2,1)}), bf16[2,128,16,128]{3,1,0,2:T(8,128)(2,1)S(1)}, u32[]{:S(2)}, u32[]{:S(2)}) async-start(bf16[2,128,16,128]{3,1,0,2:T(8,128)(2,1)} %copy.152), calls=%async_computation.1 | async-start | bytes 2097152 | tf_op jit(solution)/shard_map/all_to_all | solution.py:173
  187.1 7.2 %copy-start.27 = (f32[16,2,128]{2,0,1:T(8,128)}, f32[16,2,128]{2,0,1:T(8,128)S(1)}, u32[]{:S(2)}) copy-start(f32[16,2,128]{2,0,1:T(8,128)S(1)} %reduce_window_sum.38) | copy-start | bytes 49156
  188.7 19.8 %copy-start.4 = (bf16[1,1024,512]{2,1,0:T(8,128)(2,1)S(1)}, bf16[1,1024,512]{2,1,0:T(8,128)(2,1)}, u32[]{:S(2)}) copy-start(bf16[1,1024,512]{2,1,0:T(8,128)(2,1)} %reshape.684) | copy-start | bytes 3145732
  211.5 6.4 %copy-start.56 = (f32[2]{0:T(128)S(1)}, f32[2]{0:T(128)}, u32[]{:S(2)}) copy-start(f32[2]{0:T(128)} %get-tuple-element.61) | copy-start | bytes 28
  232.4 9.0 %copy-start.23 = (f32[1,2,64,128]{3,2,1,0:T(8,128)S(1)}, f32[1,2,64,128]{3,2,1,0:T(8,128)}, u32[]{:S(2)}) copy-start(f32[1,2,64,128]{3,2,1,0:T(8,128)} %get-tuple-element.135) | copy-start | bytes 196612
  232.4 9.0 %copy-start.24 = (f32[1,2,64,128]{3,2,1,0:T(8,128)S(1)}, f32[1,2,64,128]{3,2,1,0:T(8,128)}, u32[]{:S(2)}) copy-start(f32[1,2,64,128]{3,2,1,0:T(8,128)} %get-tuple-element.137) | copy-start | bytes 196612
  234.6 58.5 %all-to-all-start.6 = ((bf16[2,2048,1,128]{3,0,2,1:T(2,128)(2,1)}), bf16[2,2048,1,128]{3,0,2,1:T(2,128)(2,1)S(1)}, u32[]{:S(2)}, u32[]{:S(2)}) async-start(bf16[2,2048,1,128]{3,0,2,1:T(2,128)(2,1)} %copy.192), calls=%async_computation.6 | async-start | bytes 2097152 | tf_op jit(solution)/shard_map/all_to_all | solution.py:206
  241.4 84.4 %all-gather.6.cloned.1.call-start = ((), (), s32[]{:S(2)}) async-start(), calls=%async_computation.9 | async-start | bytes 1179648 | tf_op jit(solution)/shard_map/all_gather | solution.py:204
  293.2 32.6 %copy-start.26 = (f32[16,1024]{1,0:T(8,128)S(1)}, f32[16,1024]{1,0:T(8,128)}, u32[]{:S(2)}) copy-start(f32[16,1024]{1,0:T(8,128)} %get-tuple-element.21) | copy-start | bytes 196612
  293.2 32.6 %copy-start.9 = (bf16[2,1024,128]{2,1,0:T(8,128)(2,1)S(1)}, bf16[2,1024,128]{2,1,0:T(8,128)(2,1)}, u32[]{:S(2)}) copy-start(bf16[2,1024,128]{2,1,0:T(8,128)(2,1)} %param.28) | copy-start | bytes 1572868
  294.4 51.7 %all-to-all-start.7 = ((bf16[2,128,2,8,128]{4,1,2,0,3:T(8,128)(2,1)}), bf16[2,128,2,8,128]{4,1,2,0,3:T(8,128)(2,1)S(1)}, u32[]{:S(2)}, u32[]{:S(2)}) async-start(bf16[2,128,2,8,128]{4,1,2,0,3:T(8,128)(2,1)} %copy.194), calls=%async_computation.7 | async-start | bytes 2097152 | tf_op jit(solution)/shard_map/all_to_all | solution.py:208
  (79 other events, 289.1 us)
Sparse Core Ops, SparseCore 0:
  10.2 44.3 all-gather.3
  56.8 55.1 all-gather.7
  267.5 50.2 all-gather.5
where the time goes:
time: 361 us; the launch traced here: 355 us
  local copies, waits for them, and re-layouts  111 us (31%)
  starting transfers between devices  73 us (20%)
  Pallas kernels  53.5 us (15%)
  other arithmetic  39.1 us (11%)
  matrix products  33.6 us (9%)
  waiting for transfers between devices  25.3 us (7%)
  between operations  19.4 us (5%)
    pallas_call x2, Pallas kernels, response_attention(): pl.pallas_call(kernel, grid_spec=grid_spec, out_shape=jax.ShapeDtypeStruc...  53.5 us
    all_to_all x1, starting transfers between devices, body(): back = lax.all_to_all(back, 'resp', 3, 3, tiled=True)  31.4 us
    another operation x8, local copies, waits for them, and re-layouts, chunked_pass(): xs = inputs.reshape(blocks, QS, heads, SP).transpose(0, 2, 1, 3)  30.1 us
    unnamed x194, local copies, waits for them, and re-layouts  11.3 us
    all_to_all x1, waiting for transfers between devices, body(): spread_x = lax.all_to_all(spread_x, 'resp', 3, 3, tiled=True)  11.2 us
    all_to_all x1, waiting for transfers between devices, body(): lax.all_to_all(spread_keys, 'seq', split_axis=2, concat_axis=1, tiled=True)  10.3 us
    dot_general x4, matrix products, chunked_pass(): jnp.einsum('ctn,chpn->chtp', cs.astype(jnp.float32), before, precision=la...  9.34 us
    dot_general x4, matrix products, chunked_pass(): jnp.einsum('chtu,chup->chtp', mixing, xs, preferred_element_type=jnp.floa...  7.92 us
  transfers between devices with their start and end apart: 11, of which 3 were waited for; matrix products, arithmetic and copies ran while one was open for 44% of the time, Pallas kernels for 15%

commit v1 on v0

--- a/solution.py
+++ b/solution.py
@@ -157,9 +157,8 @@
     spread_values = jnp.repeat(
         prompt_values.reshape(prompt_count, shard_rows, memory_head_number, HDIM), repeat, axis=2
     ).reshape(prompt_count, shard_rows, seq_count * HDIM)
-    moved_keys, moved_values = (
-        lax.all_to_all(spread_keys, "seq", split_axis=2, concat_axis=1, tiled=True),
-        lax.all_to_all(spread_values, "seq", split_axis=2, concat_axis=1, tiled=True),
+    moved_pair = lax.all_to_all(
+        jnp.stack([spread_keys, spread_values]), "seq", split_axis=3, concat_axis=2, tiled=True
     )
     resp_rates = lax.dynamic_slice_in_dim(ssm_rate, seq_index * resp_heads, resp_heads)
     resp_count = lax.axis_size("resp")
@@ -167,14 +166,34 @@
     halves = seq_count // resp_count
     width = heads_per_chain * SP
     shard_rows = prompt_x.shape[1]
+    own_head = seq_index // repeat
+
+    def local_pass(item, inputs):
+        return chunked_pass(inputs[item], resp_dt[item], resp_b[item], resp_c[item], resp_rates)
+
+    resp_locals = [local_pass(0, resp_x)]
+    moved_pair, resp_locals = lax.optimization_barrier((moved_pair, resp_locals))
+    attention_args = (
+        moved_pair[0], moved_pair[1], resp_keys, resp_values, resp_group, resp_len, own_head
+    )
     spread_x = prompt_x.reshape(prompt_count, shard_rows, halves, resp_count, width)
     spread_x = lax.all_to_all(spread_x, "resp", 3, 3, tiled=True)
+    outs = [response_attention(resp_query, *attention_args, 0)]
+    spread_x, outs, resp_x, prompt_dt = lax.optimization_barrier((spread_x, outs, resp_x, prompt_dt))
+    spread_dt = prompt_dt.reshape(prompt_count, halves, resp_count, heads_per_chain, shard_rows)
+    spread_dt = lax.all_to_all(spread_dt, "resp", 2, 2, tiled=True)
+    for item in range(1, responses_here):
+        resp_locals.append(local_pass(item, resp_x))
+    spread_dt, resp_locals, resp_query = lax.optimization_barrier(
+        (spread_dt, resp_locals, resp_query)
+    )
     spread_x = spread_x.transpose(0, 1, 3, 2, 4).reshape(prompt_count, shard_rows, seq_count, width)
     chain_x = lax.all_to_all(spread_x, "seq", 2, 1, tiled=True).reshape(
         prompt_count, shard_rows * seq_count, width
     )
-    spread_dt = prompt_dt.reshape(prompt_count, halves, resp_count, heads_per_chain, shard_rows)
-    spread_dt = lax.all_to_all(spread_dt, "resp", 2, 2, tiled=True)
+    for item in range(1, responses_here):
+        outs.append(response_attention(resp_query, *attention_args, item))
+    chain_x, outs, spread_dt = lax.optimization_barrier((chain_x, outs, spread_dt))
     spread_dt = spread_dt.transpose(0, 2, 1, 3, 4).reshape(
         prompt_count, seq_count, heads_per_chain, shard_rows
     )
@@ -183,12 +202,6 @@
     )
     chain_b = lax.all_gather(prompt_b, "seq", axis=1, tiled=True)
     chain_c = lax.all_gather(prompt_c, "seq", axis=1, tiled=True)
-    own_head = seq_index // repeat
-    attention_args = (moved_keys, moved_values, resp_keys, resp_values, resp_group, resp_len, own_head)
-    outs = []
-    for item in range(responses_here):
-        outs.append(response_attention(resp_query, *attention_args, item))
-    chain_x, chain_dt, outs = lax.optimization_barrier((chain_x, chain_dt, outs))
     chain_rates = lax.dynamic_slice_in_dim(
         ssm_rate, seq_index * resp_heads + resp_index * heads_per_chain, heads_per_chain
     )
@@ -200,19 +213,13 @@
         )
         chain_outs.append(head_norm(out).astype(jnp.bfloat16))
         chain_finals.append(final)
-    chain_final, resp_x = lax.optimization_barrier((jnp.stack(chain_finals), resp_x))
+    chain_final = jnp.stack(chain_finals)
     start_states = lax.all_gather(chain_final, "resp", axis=1, tiled=True)
     back = jnp.stack(chain_outs).reshape(prompt_count, shard_rows * seq_count, 1, width)
     back = lax.all_to_all(back, "seq", 1, 2, tiled=True)
     back = back.reshape(prompt_count, shard_rows, resp_count, halves, width).transpose(0, 1, 3, 2, 4)
     back = lax.all_to_all(back, "resp", 3, 3, tiled=True)
     prompt_ssm_out = back.reshape(prompt_count, shard_rows, halves * resp_count * width)
-    resp_locals = []
-    for item in range(responses_here):
-        resp_locals.append(
-            chunked_pass(resp_x[item], resp_dt[item], resp_b[item], resp_c[item], resp_rates)
-        )
-    start_states, resp_locals = lax.optimization_barrier((start_states, resp_locals))
     resp_attn_out = jnp.concatenate(outs, axis=0)
     positions = lax.broadcasted_iota(jnp.int32, (slots,), 0)
     resp_outs = []

time: 361 us -> 357 us (0.989)
  the two profiles are of different devices: /device:TPU:1 before, /device:TPU:33 now
where the time goes in v1:
time: 357 us; the launch traced here: 352 us
  local copies, waits for them, and re-layouts  93.8 us (26%)
  other arithmetic  65.7 us (18%)
  starting transfers between devices  61.7 us (17%)
  Pallas kernels  57.9 us (16%)
  matrix products  44 us (12%)
  between operations  18.7 us (5%)
  waiting for transfers between devices  9.81 us (3%)
    pallas_call x2, Pallas kernels, response_attention(): pl.pallas_call(kernel, grid_spec=grid_spec, out_shape=jax.ShapeDtypeStruc...  57.9 us
    unnamed x40, other arithmetic  36.5 us
    another operation x8, local copies, waits for them, and re-layouts, chunked_pass(): xs = inputs.reshape(blocks, QS, heads, SP).transpose(0, 2, 1, 3)  23.1 us
    all_to_all x1, starting transfers between devices, body(): spread_dt = lax.all_to_all(spread_dt, 'resp', 2, 2, tiled=True)  16.3 us
    dot_general x4, matrix products, chunked_pass(): jnp.einsum('ctn,chpn->chtp', cs.astype(jnp.float32), before, precision=la...  15.4 us
    dot_general x4, matrix products, chunked_pass(): jnp.einsum('chtu,chup->chtp', mixing, xs, preferred_element_type=jnp.floa...  12.9 us
    all_to_all x1, starting transfers between devices, body(): back = lax.all_to_all(back, 'resp', 3, 3, tiled=True)  11.4 us
    reshape x4, local copies, waits for them, and re-layouts, chunked_pass(): output = output.transpose(0, 2, 1, 3).reshape(window_extent, heads, SP)  10.2 us
  transfers between devices with their start and end apart: 10, of which 2 were waited for; matrix products, arithmetic and copies ran while one was open for 45% of the time, Pallas kernels for 16%

profile of v1, /device:TPU:33, one launch (start us, length us, event | category | flops | bytes accessed | tf_op | source)
XLA Modules:
  0.0 351.6 jit_solution(17940950287386392619)
XLA Ops:
  12.2 3.9 %pad_maximum_fusion.1 = bf16[2,2,128,2048]{2,1,0,3:T(2,128)(2,1)} fusion(bf16[1,2,128,2048]{2,1,0,3:T(2,128)(2,1)S(1)} %bitcast.386, bf16[1,2,128,2048]{2,1,0,3:T(2,128)(2,1)S(1)} %bitcast.385), kind=kLoop, calls=%fused_computation.37 | loop fusion | flops 1048576 | bytes 4194304 | tf_op jit(solution)/shard_map/stack | solution.py:161
  16.0 6.9 %all-to-all-start.1 = ((bf16[2,2,128,2048]{2,1,0,3:T(2,128)(2,1)}), bf16[2,2,128,2048]{2,1,0,3:T(2,128)(2,1)}, u32[]{:S(2)}, u32[]{:S(2)}) async-start(bf16[2,2,128,2048]{2,1,0,3:T(2,128)(2,1)} %pad_maximum_fusion.1), calls=%async_computation.1 | async-start | bytes 4194304 | tf_op jit(solution)/shard_map/all_to_all | solution.py:160
  30.8 3.9 %reshape.711 = bf16[8,128,16,64]{3,2,1,0:T(8,128)(2,1)} reshape(bf16[1,1024,1024]{2,1,0:T(8,128)(2,1)S(1)} %slice-done) | data formatting | bytes 4194304 | tf_op jit(solution)/shard_map/reshape;squeeze | solution.py:76
  34.8 5.0 %copy.153 = bf16[8,128,16,64]{1,3,2,0:T(8,128)(2,1)S(1)} copy(bf16[8,128,16,64]{3,2,1,0:T(8,128)(2,1)} %reshape.711) | data formatting | bytes 4194304 | tf_op jit(solution)/shard_map/reshape;squeeze | solution.py:76
  43.5 3.1 fusion
  66.6 6.4 %all-to-all-start = ((bf16[2,128,2,8,128]{1,4,2,0,3:T(8,128)(2,1)}), bf16[2,128,2,8,128]{1,4,2,0,3:T(8,128)(2,1)S(1)}, u32[]{:S(2)}, u32[]{:S(2)}) async-start(bf16[2,128,2,8,128]{1,4,2,0,3:T(8,128)(2,1)} %copy.146), calls=%async_computation | async-start | bytes 2097152 | tf_op jit(solution)/shard_map/all_to_all | solution.py:180
  73.0 3.2 copy.149
  76.2 3.0 copy.150
  80.7 27.0 %shard_map.175 = bf16[1,4096,128]{2,1,0:T(8,128)(2,1)} custom-call(s32[2]{0:T(128)} %group_ref.3, s32[2]{0:T(128)} %len_ref.3, s32[1]{0:T(128)} %bitcast.1.head_ref, bf16[2,4096,128]{2,1,0:T(8,128)(2,1)} %reshape.680.q_ref, bf16[2,2048,128]{2,1,0:T(8,128)(2,1)} %get-tuple-element.145.pk_ref, bf16[2,2048,128]{2,1,0:T(8,128)(2,1)} %get-tuple-element.144.pv_ref, ...), custom_call_target="tpu_custom_call" | custom-call | flops 6442450944 | bytes 3670016 | tf_op jit(solution)/shard_map/pallas_call | solution.py:303
  107.7 2.7 reshape.685
  110.4 3.9 %reshape.712 = bf16[8,128,16,64]{3,2,1,0:T(8,128)(2,1)} reshape(bf16[1,1024,1024]{2,1,0:T(8,128)(2,1)S(1)} %slice-done.1) | data formatting | bytes 4194304 | tf_op jit(solution)/shard_map/reshape;squeeze | solution.py:76
  114.4 4.9 %copy.162 = bf16[8,128,16,64]{1,3,2,0:T(8,128)(2,1)S(1)} copy(bf16[8,128,16,64]{3,2,1,0:T(8,128)(2,1)} %reshape.712) | data formatting | bytes 4194304 | tf_op jit(solution)/shard_map/reshape;squeeze | solution.py:76
  120.7 16.3 %all-to-all-start.3 = ((f32[2,2,8,2,128]{4,1,3,0,2:T(2,128)}), f32[2,2,8,2,128]{4,1,3,0,2:T(2,128)}, u32[]{:S(2)}, u32[]{:S(2)}) async-start(f32[2,2,8,2,128]{4,1,3,0,2:T(2,128)} %copy.159), calls=%async_computation.3 | async-start | bytes 65536 | tf_op jit(solution)/shard_map/all_to_all | solution.py:184
  147.7 6.8 %fusion.1 = f32[8,16,128,64]{2,3,1,0:T(8,128)} fusion(f32[8,16,128]{2,1,0:T(8,128)} %bitcast.407, f32[8,128,128]{2,1,0:T(8,128)S(1)} %copy-done.19, f32[8,16,128]{2,1,0:T(8,128)S(1)} %reduce_window_sum.40, pred[128,128]{1,0:T(8,128)(4,1)S(1)} %iota_compare_fusion, bf16[8,128,16,64]{1,3,2,0:T(8,128)(2,1)S(1)} %copy.162), kind=kOutput, calls=%fused_computation.3 | convolution fusion | flops 278921216 | bytes 6963200 | tf_op jit(solution)/shard_map/chtu,chup->chtp/dot_general | solution.py:89
  155.8 7.8 %fusion.5 = f32[8,16,8,8,128]{4,3,2,1,0:T(8,128)} fusion(f32[8,16,128,64]{2,3,1,0:T(8,128)} %fusion.1, f32[8,16,64,128]{3,2,1,0:T(8,128)} %fusion.48, bf16[8,128,128,1]{2,1,3,0:T(8,128)(2,1)S(1)} %bitcast.388, f32[8,128,16]{1,2,0:T(8,128)S(1)} %get-tuple-element.162), kind=kOutput, calls=%fused_computation.13 | convolution fusion | flops 1612709888 | bytes 12910592 | tf_op jit(solution)/shard_map/ctn,chpn->chtp/dot_general | solution.py:106
  167.2 7.1 %all-to-all-start.2 = ((bf16[2,128,16,128]{3,1,0,2:T(8,128)(2,1)}), bf16[2,128,16,128]{3,1,0,2:T(8,128)(2,1)}, u32[]{:S(2)}, u32[]{:S(2)}) async-start(bf16[2,128,16,128]{3,1,0,2:T(8,128)(2,1)} %copy.157), calls=%async_computation.2 | async-start | bytes 2097152 | tf_op jit(solution)/shard_map/all_to_all | solution.py:191
  175.9 4.9 %copy.230 = f32[8,16,8,8,128]{4,3,0,2,1:T(8,128)} copy(f32[8,16,8,8,128]{4,3,2,1,0:T(8,128)} %fusion.5) | data formatting | bytes 8388608 | tf_op jit(solution)/shard_map/reshape | solution.py:111
  184.8 31.0 %shard_map.176 = bf16[1,4096,128]{2,1,0:T(8,128)(2,1)} custom-call(s32[2]{0:T(128)} %group_ref.3, s32[2]{0:T(128)} %len_ref.3, s32[1]{0:T(128)} %bitcast.1.head_ref, bf16[2,4096,128]{2,1,0:T(8,128)(2,1)} %reshape.691.q_ref, bf16[2,2048,128]{2,1,0:T(8,128)(2,1)} %get-tuple-element.145.pk_ref, bf16[2,2048,128]{2,1,0:T(8,128)(2,1)} %get-tuple-element.144.pv_ref, ...), custom_call_target="tpu_custom_call" | custom-call | flops 6442450944 | bytes 3670016 | tf_op jit(solution)/shard_map/pallas_call | solution.py:303
  221.0 6.8 %all-to-all-start.4 = ((f32[2,16,2,128]{3,2,0,1:T(2,128)}), f32[2,16,2,128]{3,2,0,1:T(2,128)S(1)}, u32[]{:S(2)}, u32[]{:S(2)}) async-start(f32[2,16,2,128]{3,2,0,1:T(2,128)} %copy.166), calls=%async_computation.4 | async-start | bytes 65536 | tf_op jit(solution)/shard_map/all_to_all | solution.py:200
  287.6 6.5 %all-to-all-start.5 = ((bf16[2,2048,1,128]{3,0,2,1:T(2,128)(2,1)}), bf16[2,2048,1,128]{3,0,2,1:T(2,128)(2,1)S(1)}, u32[]{:S(2)}, u32[]{:S(2)}) async-start(bf16[2,2048,1,128]{3,0,2,1:T(2,128)(2,1)} %copy.186), calls=%async_computation.5 | async-start | bytes 2097152 | tf_op jit(solution)/shard_map/all_to_all | solution.py:219
  301.7 8.3 %all-to-all-done.5 = bf16[2,2048,1,128]{3,0,2,1:T(2,128)(2,1)S(1)} async-done(((bf16[2,2048,1,128]{3,0,2,1:T(2,128)(2,1)}), bf16[2,2048,1,128]{3,0,2,1:T(2,128)(2,1)S(1)}, u32[]{:S(2)}, u32[]{:S(2)}) %all-to-all-start.5) | async-done | bytes 1048608 | tf_op jit(solution)/shard_map/all_to_all | solution.py:219
  311.3 11.4 %all-to-all-start.6 = ((bf16[2,128,2,8,128]{4,1,2,0,3:T(8,128)(2,1)}), bf16[2,128,2,8,128]{4,1,2,0,3:T(8,128)(2,1)S(1)}, u32[]{:S(2)}, u32[]{:S(2)}) async-start(bf16[2,128,2,8,128]{4,1,2,0,3:T(8,128)(2,1)} %copy.188), calls=%async_computation.6 | async-start | bytes 2097152 | tf_op jit(solution)/shard_map/all_to_all | solution.py:221
  322.7 4.8 %multiply_reduce_fusion.1 = (f32[1024,16]{0,1:T(8,128)S(1)}, f32[1024,16,64]{0,2,1:T(8,128)S(1)}) fusion(f32[1024,16,64]{0,2,1:T(8,128)} %bitcast.366, bf16[2,1024,128]{2,1,0:T(8,128)(2,1)S(1)} %copy-done.14, f32[2,16,64,128]{3,2,1,0:T(8,128)} %all-gather.6.cloned.1.call-done, s32[]{:T(128)S(6)} %select_n.58, f32[1024,16]{0,1:T(8,128)S(1)} %get-tuple-element.203), kind=kOutput, calls=%fused_computation.20 | convolution fusion | flops 1614790656 | bytes 9306116 | tf_op jit(solution)/shard_map/tn,hdn->thd/dot_general | solution.py:229
  335.1 2.9 copy.175
  (275 shorter events, 144.4 us)
Async XLA Ops:
  7.2 138.3 %all-gather.4.cloned.1.call-start = ((), (), s32[]{:S(2)}) async-start(), calls=%async_computation.7 | async-start | bytes 1114112 | tf_op jit(solution)/shard_map/all_gather | solution.py:203
  12.2 11.6 %copy-start.25 = (f32[2,16,1024]{2,1,0:T(8,128)S(1)}, f32[2,16,1024]{2,1,0:T(8,128)}, u32[]{:S(2)}) copy-start(f32[2,16,1024]{2,1,0:T(8,128)} %param.26) | copy-start | bytes 393220
  12.2 11.7 %copy-start.44 = (f32[256]{0:T(256)S(1)}, f32[256]{0:T(256)}, u32[]{:S(2)}) copy-start(f32[256]{0:T(256)} %param.29) | copy-start | bytes 3076
  16.0 14.7 %copy-start.18 = (bf16[2,1024,128]{2,1,0:T(8,128)(2,1)S(1)}, bf16[2,1024,128]{2,1,0:T(8,128)(2,1)}, u32[]{:S(2)}) copy-start(bf16[2,1024,128]{2,1,0:T(8,128)(2,1)} %param.27) | copy-start | bytes 1572868
  16.0 50.5 %all-to-all-start.1 = ((bf16[2,2,128,2048]{2,1,0,3:T(2,128)(2,1)}), bf16[2,2,128,2048]{2,1,0,3:T(2,128)(2,1)}, u32[]{:S(2)}, u32[]{:S(2)}) async-start(bf16[2,2,128,2048]{2,1,0,3:T(2,128)(2,1)} %pad_maximum_fusion.1), calls=%async_computation.1 | async-start | bytes 4194304 | tf_op jit(solution)/shard_map/all_to_all | solution.py:160
  23.0 131.5 %all-gather.8.cloned.1.call-start = ((), (), s32[]{:S(2)}) async-start(), calls=%async_computation.9 | async-start | bytes 1114112 | tf_op jit(solution)/shard_map/all_gather | solution.py:204
  30.8 34.6 %copy-start.13 = (bf16[1,1024,128]{2,1,0:T(8,128)(2,1)}, bf16[1,1024,128]{2,1,0:T(8,128)(2,1)S(1)}, u32[]{:S(2)}) copy-start(bf16[1,1024,128]{2,1,0:T(8,128)(2,1)S(1)} %get-tuple-element.156) | copy-start | bytes 786436
  66.6 43.8 %all-to-all-start = ((bf16[2,128,2,8,128]{1,4,2,0,3:T(8,128)(2,1)}), bf16[2,128,2,8,128]{1,4,2,0,3:T(8,128)(2,1)S(1)}, u32[]{:S(2)}, u32[]{:S(2)}) async-start(bf16[2,128,2,8,128]{1,4,2,0,3:T(8,128)(2,1)} %copy.146), calls=%async_computation | async-start | bytes 2097152 | tf_op jit(solution)/shard_map/all_to_all | solution.py:180
  119.3 19.4 %copy-start.30 = (f32[16]{0:T(128)S(1)}, f32[16]{0:T(128)}, u32[]{:S(2)}) copy-start(f32[16]{0:T(128)} %get-tuple-element.180) | copy-start | bytes 196
  119.3 20.3 %copy-start.42 = (f32[16]{0:T(128)S(1)}, f32[16]{0:T(128)}, u32[]{:S(2)}) copy-start(f32[16]{0:T(128)} %get-tuple-element.179) | copy-start | bytes 196
  120.7 46.5 %all-to-all-start.3 = ((f32[2,2,8,2,128]{4,1,3,0,2:T(2,128)}), f32[2,2,8,2,128]{4,1,3,0,2:T(2,128)}, u32[]{:S(2)}, u32[]{:S(2)}) async-start(f32[2,2,8,2,128]{4,1,3,0,2:T(2,128)} %copy.159), calls=%async_computation.3 | async-start | bytes 65536 | tf_op jit(solution)/shard_map/all_to_all | solution.py:184
  167.2 51.0 %all-to-all-start.2 = ((bf16[2,128,16,128]{3,1,0,2:T(8,128)(2,1)}), bf16[2,128,16,128]{3,1,0,2:T(8,128)(2,1)}, u32[]{:S(2)}, u32[]{:S(2)}) async-start(bf16[2,128,16,128]{3,1,0,2:T(8,128)(2,1)} %copy.157), calls=%async_computation.2 | async-start | bytes 2097152 | tf_op jit(solution)/shard_map/all_to_all | solution.py:191
  221.0 13.2 %all-to-all-start.4 = ((f32[2,16,2,128]{3,2,0,1:T(2,128)}), f32[2,16,2,128]{3,2,0,1:T(2,128)S(1)}, u32[]{:S(2)}, u32[]{:S(2)}) async-start(f32[2,16,2,128]{3,2,0,1:T(2,128)} %copy.166), calls=%async_computation.4 | async-start | bytes 65536 | tf_op jit(solution)/shard_map/all_to_all | solution.py:200
  227.8 94.9 %all-gather.6.cloned.1.call-start = ((), (), s32[]{:S(2)}) async-start(), calls=%async_computation.8 | async-start | bytes 1179648 | tf_op jit(solution)/shard_map/all_gather | solution.py:217
  234.0 13.4 %copy-start.15 = (bf16[16,128,2,64]{1,3,2,0:T(8,128)(2,1)S(1)}, bf16[16,128,2,64]{1,3,2,0:T(8,128)(2,1)}, u32[]{:S(2)}) copy-start(bf16[16,128,2,64]{1,3,2,0:T(8,128)(2,1)} %copy.169) | copy-start | bytes 1572868
  235.5 11.9 %copy-start.17 = (f32[16,128,128]{2,1,0:T(8,128)S(1)}, f32[16,128,128]{2,1,0:T(8,128)}, u32[]{:S(2)}) copy-start(f32[16,128,128]{2,1,0:T(8,128)} %fusion.83) | copy-start | bytes 3145732
  285.3 13.0 %copy-start.41 = (s32[2]{0:T(128)S(1)}, s32[2]{0:T(128)}, u32[]{:S(2)}) copy-start(s32[2]{0:T(128)} %len_ref.3) | copy-start | bytes 28
  285.3 14.8 %copy-start.22 = (f32[16,1024]{1,0:T(8,128)S(1)}, f32[16,1024]{1,0:T(8,128)}, u32[]{:S(2)}) copy-start(f32[16,1024]{1,0:T(8,128)} %copy_bitcast_fusion.3) | copy-start | bytes 196612
  285.3 14.8 %copy-start.23 = (f32[16,1024]{1,0:T(8,128)S(1)}, f32[16,1024]{1,0:T(8,128)}, u32[]{:S(2)}) copy-start(f32[16,1024]{1,0:T(8,128)} %copy_bitcast_fusion.2) | copy-start | bytes 196612
  285.3 14.9 %copy-start.11 = (bf16[1,1024,512]{2,1,0:T(8,128)(2,1)S(1)}, bf16[1,1024,512]{2,1,0:T(8,128)(2,1)}, u32[]{:S(2)}) copy-start(bf16[1,1024,512]{2,1,0:T(8,128)(2,1)} %reshape.685) | copy-start | bytes 3145732
  285.3 14.9 %copy-start.12 = (bf16[1,1024,512]{2,1,0:T(8,128)(2,1)S(1)}, bf16[1,1024,512]{2,1,0:T(8,128)(2,1)}, u32[]{:S(2)}) copy-start(bf16[1,1024,512]{2,1,0:T(8,128)(2,1)} %reshape.692) | copy-start | bytes 3145732
  287.6 22.5 %all-to-all-start.5 = ((bf16[2,2048,1,128]{3,0,2,1:T(2,128)(2,1)}), bf16[2,2048,1,128]{3,0,2,1:T(2,128)(2,1)S(1)}, u32[]{:S(2)}, u32[]{:S(2)}) async-start(bf16[2,2048,1,128]{3,0,2,1:T(2,128)(2,1)} %copy.186), calls=%async_computation.5 | async-start | bytes 2097152 | tf_op jit(solution)/shard_map/all_to_all | solution.py:219
  301.7 20.9 %copy-start.14 = (bf16[2,1024,128]{2,1,0:T(8,128)(2,1)S(1)}, bf16[2,1024,128]{2,1,0:T(8,128)(2,1)}, u32[]{:S(2)}) copy-start(bf16[2,1024,128]{2,1,0:T(8,128)(2,1)} %param.28) | copy-start | bytes 1572868
  311.3 31.6 %all-to-all-start.6 = ((bf16[2,128,2,8,128]{4,1,2,0,3:T(8,128)(2,1)}), bf16[2,128,2,8,128]{4,1,2,0,3:T(8,128)(2,1)S(1)}, u32[]{:S(2)}, u32[]{:S(2)}) async-start(bf16[2,128,2,8,128]{4,1,2,0,3:T(8,128)(2,1)} %copy.188), calls=%async_computation.6 | async-start | bytes 2097152 | tf_op jit(solution)/shard_map/all_to_all | solution.py:221
  (34 other events, 195.8 us)
Sparse Core Ops, SparseCore 0:
  10.2 60.9 all-gather.3
  73.4 41.8 all-gather.7
  274.8 32.1 all-gather.5
